TPU v7x, 128 devices: a whole 4x4x4 slice. The times are simulated.
128 devices in a mesh: tm: 32 (over x, z_hi, y), qband: 4 (over z_lo, core).
Axes of the slice: x: 4, y: 4, z: 4 (z_hi: 2, z_lo: 2; z = z_hi * 2 + z_lo), core: 2. Of those that a mesh axis runs over, the one named last changes fastest.
Arguments:
- frames: bfloat16 [128, 1024, 1024], P(('tm', 'qband')), may hold values from -8 to 8
- lag_list: int32 [16], replicated, may hold values from 1 to 64, as said below
- band_index: int32 [1024, 1], P(('tm', 'qband')), may hold values from 0 to 63
- decay_rates: float32 [64, 1024], P('tm', 'qband'), may hold values from 0.002 to 1
Outputs:
- structure: float32 [16, 1024, 1024], P(None, ('tm', 'qband'))
- weights: float32 [64, 1024], P('tm', 'qband')
Inputs may be any that keep to these rules, and one draw needn't show every extreme that they name: `lag_list`: 16 different lags, the largest exactly 64. `band_index`: every band has at least one row.
All inputs are finite; a program needn't handle non-finite values.
Results may differ from a plain program's by a relative error of at most 0.0018.
Values may be sent and summed in bfloat16 or wider, within the bound.
No kernel may reach another device: no remote copies, remote signals or barrier semaphores. Data moves between devices by JAX's collectives and lax.ppermute only.
A program may use at most 128 MiB of HBM per device.

v0:
```python
import math
import jax
import jax.numpy as jnp
from jax import lax
from jax.sharding import PartitionSpec as P

BINS = 1024
ITERS = 64


def dft_table(length):
    positions = jnp.arange(length, dtype=jnp.int32)
    phase_index = positions[:, None] * positions[None, :] % length
    folded = jnp.minimum(phase_index, length - phase_index)
    sign_factor = jnp.where(phase_index * 2 > length, -1.0, 1.0).astype(jnp.float32)
    angles = folded.astype(jnp.float32) * (2.0 * math.pi / length)
    factor = 1.0 / math.sqrt(length)
    return jnp.concatenate(
        [jnp.cos(angles) * factor, -sign_factor * jnp.sin(angles) * factor], axis=1
    ).astype(jnp.bfloat16)


def structure_block(spectrum_block, lag_list):
    frames_all = spectrum_block.shape[2]
    padded = jnp.concatenate([spectrum_block, jnp.zeros_like(spectrum_block)], axis=2)
    time_index = jnp.arange(frames_all, dtype=jnp.int32)

    def one_lag(lag_value):
        shifted = lax.dynamic_slice_in_dim(padded, lag_value, frames_all, 2)
        difference = shifted.astype(jnp.float32) - spectrum_block.astype(jnp.float32)
        squared = difference[0] * difference[0] + difference[1] * difference[1]
        in_range = (time_index < frames_all - lag_value).astype(jnp.float32)
        summed = jnp.sum(squared * in_range[None, :, None], axis=1)
        return summed / (frames_all - lag_value).astype(jnp.float32)

    return lax.map(one_lag, lag_list)


def kernel_panel(decay_rates, lag_list):
    lag_values = lag_list.astype(jnp.float32)
    return (1.0 - jnp.exp(-decay_rates[:, None, :] * lag_values[None, :, None])) / BINS


def descend(kernel, target, step_size, weights, combine):
    partial_value = jnp.einsum("blk,bk->bl", kernel, weights, precision=lax.Precision.HIGHEST)
    residual = combine(partial_value) - target
    gradient = jnp.einsum("blk,bl->bk", kernel, residual, precision=lax.Precision.HIGHEST)
    return jnp.maximum(weights - step_size[:, None] * gradient, 0.0)


def on_device(frames, lag_list, band_index, decay_rates):
    frames_dev, pixels = (frames.shape[0], frames.shape[1])
    table = dft_table(pixels)
    row_transform = jnp.einsum("xk,tyx->kty", table, frames, preferred_element_type=jnp.float32)
    row_transform = row_transform.reshape(2, pixels, frames_dev, pixels).astype(jnp.bfloat16)
    products = jnp.einsum("ckty,yj->cktj", row_transform, table, preferred_element_type=jnp.float32)
    spec_real = products[0, :, :, :pixels] - products[1, :, :, pixels:]
    spec_imag = products[0, :, :, pixels:] + products[1, :, :, :pixels]
    spectrum = jnp.stack([spec_real, spec_imag]).astype(jnp.bfloat16)
    structure = structure_block(
        lax.all_to_all(spectrum, ("tm", "qband"), split_axis=1, concat_axis=2, tiled=True), lag_list
    )
    bands_dev = decay_rates.shape[0]
    bands_total = bands_dev * lax.axis_size("tm")
    row_sums = jnp.sum(structure, axis=2)
    band_ids = jnp.arange(bands_total, dtype=jnp.int32)
    one_hot = (band_index[:, 0][None, :] == band_ids[:, None]).astype(jnp.float32)
    partial_totals = jnp.dot(one_hot, row_sums.T, precision=lax.Precision.HIGHEST)
    partial_counts = jnp.sum(one_hot, axis=1)
    totals, counts = lax.psum((partial_totals, partial_counts), ("tm", "qband"))
    band_mean = totals / (counts[:, None] * pixels)
    target = lax.dynamic_slice_in_dim(band_mean, lax.axis_index("tm") * bands_dev, bands_dev, 0)
    columns = decay_rates.shape[1]
    kernel = kernel_panel(decay_rates, lag_list)
    norm_part = jnp.sum(kernel * kernel, axis=(1, 2))
    step_size = 1.0 / lax.psum(norm_part, "qband")

    def combine_bins(partial_value):
        return lax.psum(partial_value, "qband")

    def iterate(counter, weights):
        return descend(kernel, target, step_size, weights, combine_bins)

    weights = lax.fori_loop(0, ITERS, iterate, jnp.zeros((bands_dev, columns), jnp.float32))
    return (structure, weights)


def solution(mesh):
    placed = (P(("tm", "qband"), None, None), P(), P(("tm", "qband"), None), P("tm", "qband"))
    return jax.shard_map(
        on_device,
        mesh=mesh,
        in_specs=placed,
        out_specs=(P(None, ("tm", "qband"), None), P("tm", "qband")),
        check_vma=False,
    )
```

profile of v0, /device:TPU:1, one launch (start us, length us, event | category | flops | bytes accessed | tf_op | source)
XLA Modules:
  0.0 888.4 jit_solution(16568552919354214911)
XLA Ops:
  0.6 18.3 %multiply_convert_fusion = (bf16[1024,1024]{1,0:T(8,128)(2,1)S(1)}, bf16[1024,1024]{1,0:T(8,128)(2,1)S(1)}) fusion(), kind=kLoop, calls=%fused_computation.49 | loop fusion | flops 26214400 | bytes 4194304 | tf_op jit(solution)/shard_map/convert.3
  23.3 6.4 copy.9
  29.7 22.7 %convolution_bitcast_fusion = f32[2,1024,1,2048]{3,1,0,2:T(8,128)} fusion(bf16[1024,1024]{1,0:T(8,128)(2,1)} %copy-done.3, bf16[1024,1024]{1,0:T(8,128)(2,1)} %copy-done.4, bf16[2,1024,1024]{2,1,0:T(8,128)(2,1)} %bitcast.66, bf16[1,1024,1024]{2,1,0:T(8,128)(2,1)S(1)} %copy-done), kind=kOutput, calls=%fused_computation.32 | convolution fusion | flops 12895387648 | bytes 27262976 | tf_op jit(solution)/shard_map/ckty,yj->cktj/dot_general | solution.py:56
  52.4 6.6 fusion.30
  59.4 6.3 copy.10
  65.7 11.9 %all-to-all-start = ((bf16[2,1024,1,1024]{3,0,2,1:T(2,128)(2,1)}), bf16[2,1024,1,1024]{3,0,2,1:T(2,128)(2,1)}, u32[]{:S(2)}, u32[]{:S(2)}) async-start(bf16[2,1024,1,1024]{3,0,2,1:T(2,128)(2,1)} %copy.10), calls=%async_computation | async-start | bytes 8388608 | tf_op jit(solution)/shard_map/all_to_all | solution.py:61
  77.9 25.1 %psum.28 = f32[2]{0:T(128)S(1)} all-reduce(f32[2]{0:T(128)S(1)} %multiply_reduce_fusion), channel_id=1, replica_groups=mesh['tm'=32,'qband'=4] {'qband'}, use_global_device_ids=true, to_apply=%region_8.9 | all-reduce | flops 2 | bytes 16 | tf_op jit(solution)/shard_map/psum | solution.py:76
  103.1 27.1 %all-to-all-done = bf16[2,1024,1,1024]{3,0,2,1:T(2,128)(2,1)} async-done(((bf16[2,1024,1,1024]{3,0,2,1:T(2,128)(2,1)}), bf16[2,1024,1,1024]{3,0,2,1:T(2,128)(2,1)}, u32[]{:S(2)}, u32[]{:S(2)}) %all-to-all-start) | async-done | bytes 4194336 | tf_op jit(solution)/shard_map/all_to_all | solution.py:61
  139.1 267.7 %while.22 = (s32[]{:T(128)}, f32[16,8,1024]{2,1,0:T(8,128)S(1)}, s32[16]{0:T(128)S(1)}, bf16[2,8,256,1024]{3,2,1,0:T(8,128)(2,1)}, bf16[2,8,128,1024]{3,2,1,0:T(...) while((s32[]{:T(128)}, f32[16,8,1024]{2,1,0:T(8,128)S(1)}, s32[16]{0:T(128)S(1)}, ...), condition=%wide.region_2.3_spmd.clone, body=%wide.region_0.2_spmd.clone.sunk | while | flops 11534599 | bytes 25265328 | solution.py:36
  141.6 8.9 convert_subtract_fusion.2
  158.4 8.9 convert_subtract_fusion.2
  175.1 8.9 convert_subtract_fusion.2
  191.8 8.9 convert_subtract_fusion.2
  208.6 8.9 convert_subtract_fusion.2
  225.3 8.9 convert_subtract_fusion.2
  242.0 8.9 convert_subtract_fusion.2
  258.7 8.9 convert_subtract_fusion.2
  275.5 8.9 convert_subtract_fusion.2
  292.2 8.9 convert_subtract_fusion.2
  308.9 8.9 convert_subtract_fusion.2
  325.7 8.9 convert_subtract_fusion.2
  342.4 8.9 convert_subtract_fusion.2
  359.1 8.9 convert_subtract_fusion.2
  375.9 8.9 convert_subtract_fusion.2
  392.6 8.9 convert_subtract_fusion.2
  407.2 64.3 %all-reduce.1 = (f32[64,16]{1,0:T(8,128)S(1)}, f32[64]{0:T(128)S(1)}) all-reduce(f32[64,16]{1,0:T(8,128)S(1)} %fusion.44, f32[64]{0:T(128)S(1)} %convert_reduce_fusion), channel_id=1, replica_groups=mesh['tm'=32,'qband'=4] {'tm','qband'}, use_global_device_ids=true, to_apply=%region_4.5 | all-reduce | flops 1088 | bytes 8704 | tf_op jit(solution)/shard_map/psum | solution.py:70
  471.6 416.2 %while.23 = (s32[]{:T(128)}, f32[2,256]{1,0:T(2,128)S(1)}, f32[2]{0:T(128)S(1)}, f32[2,16]{1,0:T(2,128)S(1)}, f32[16]{0:T(128)S(1)}, /*index=5*/f32[2,256]{1,0:T(2,128)S(1)}, s32[]{:T(128)}, s32[]{:T(128)}) while((s32[]{:T(128)}, f32[2,256]{1,0:T(2,128)S(1)}, f32[2]{0:T(128)S(1)}, f32[2,16]{1,0:T(2,128)S(1)}, f32[16]{0:T(128)S(1)}, ...), condition=%wide.region_11.12_spmd.clone, body=%wide.region_9.11_spmd.clone.sunk | while | flops 248387 | bytes 19560 | solution.py:84
  484.4 5.8 psum.33
  490.7 6.6 psum.33
  504.1 6.1 psum.33
  517.0 6.1 psum.33
  529.9 6.6 psum.33
  537.0 5.8 psum.33
  555.9 6.3 psum.33
  569.1 6.3 psum.33
  582.1 5.8 psum.33
  594.8 6.5 psum.33
  601.9 5.8 psum.33
  608.2 6.1 psum.33
  621.0 6.0 psum.33
  627.6 5.8 psum.33
  634.0 6.6 psum.33
  647.4 5.8 psum.33
  659.9 6.3 psum.33
  673.1 6.3 psum.33
  686.2 5.8 psum.33
  698.8 6.6 psum.33
  705.9 5.8 psum.33
  712.3 6.0 psum.33
  725.1 6.1 psum.33
  731.7 5.8 psum.33
  738.0 6.5 psum.33
  745.1 5.8 psum.33
  751.5 5.8 psum.33
  764.0 6.3 psum.33
  770.8 5.8 psum.33
  777.2 6.3 psum.33
  796.6 5.8 psum.33
  802.9 6.6 psum.33
  816.3 6.1 psum.33
  829.1 6.1 psum.33
  842.1 6.6 psum.33
  868.0 6.3 psum.33
  881.3 6.3 psum.33
  (447 shorter events, 287.7 us)
Async XLA Ops:
  0.6 29.1 %copy-start = (bf16[1,1024,1024]{2,1,0:T(8,128)(2,1)S(1)}, bf16[1,1024,1024]{2,1,0:T(8,128)(2,1)}, u32[]{:S(2)}) copy-start(bf16[1,1024,1024]{2,1,0:T(8,128)(2,1)} %param.8) | copy-start | bytes 6291460
  19.0 1.3 copy-start.3
  19.0 2.0 copy-start.4
  65.7 12.0 %copy-start.7 = (f32[2,256]{1,0:T(2,128)S(1)}, f32[2,256]{1,0:T(2,128)}, u32[]{:S(2)}) copy-start(f32[2,256]{1,0:T(2,128)} %param.11) | copy-start | bytes 6148
  65.7 12.0 %copy-start.8 = (s32[16]{0:T(128)S(1)}, s32[16]{0:T(128)}, u32[]{:S(2)}) copy-start(s32[16]{0:T(128)} %param.9) | copy-start | bytes 196
  65.7 37.3 %copy-start.9 = (s32[8,1]{0,1:T(1,128)S(1)}, s32[8,1]{0,1:T(1,128)}, u32[]{:S(2)}) copy-start(s32[8,1]{0,1:T(1,128)} %param.10) | copy-start | bytes 100
  65.7 64.4 %all-to-all-start = ((bf16[2,1024,1,1024]{3,0,2,1:T(2,128)(2,1)}), bf16[2,1024,1,1024]{3,0,2,1:T(2,128)(2,1)}, u32[]{:S(2)}, u32[]{:S(2)}) async-start(bf16[2,1024,1,1024]{3,0,2,1:T(2,128)(2,1)} %copy.10), calls=%async_computation | async-start | bytes 8388608 | tf_op jit(solution)/shard_map/all_to_all | solution.py:61
  134.6 4.5 copy-start.2
  406.8 481.1 %copy-start.5 = (f32[16,8,1024]{2,1,0:T(8,128)}, f32[16,8,1024]{2,1,0:T(8,128)S(1)}, u32[]{:S(2)}) copy-start(f32[16,8,1024]{2,1,0:T(8,128)S(1)} %get-tuple-element.59) | copy-start | bytes 1572868
  406.8 481.6 %copy-start.1 = (bf16[1,1024,1024]{2,1,0:T(8,128)(2,1)S(1)}, bf16[1,1024,1024]{2,1,0:T(8,128)(2,1)}, u32[]{:S(2)}) copy-start(bf16[1,1024,1024]{2,1,0:T(8,128)(2,1)} %param.8) | copy-start | bytes 6291460
  887.8 0.6 copy-start.6
where the time goes:
time: 891 us; the launch traced here: 888 us
  blocking collectives  471 us (53%)
  other arithmetic  250 us (28%)
  matrix products  51.5 us (6%)
  loops' own time  42.4 us (5%)
  local copies, waits for them, and re-layouts  33.7 us (4%)
  waiting for transfers between devices  27.1 us (3%)
  starting transfers between devices  11.9 us (1%)
    psum x64, blocking collectives, combine_bins(): return lax.psum(partial_value, 'qband')  381 us
    sub x16, other arithmetic, one_lag(): shifted.astype(jnp.float32) - spectrum_block.astype(jnp.float32)  142 us
    reduce_sum x16, other arithmetic, one_lag(): summed = jnp.sum(squared * in_range[None, :, None], axis=1)  73.8 us
    psum x1, blocking collectives, on_device(): totals, counts = lax.psum((partial_totals, partial_counts), ('tm', 'qband'))  64.3 us
    another operation x1, loops' own time, structure_block(): return lax.map(one_lag, lag_list)  42.2 us
    all_to_all x1, waiting for transfers between devices, on_device(): lax.all_to_all(spectrum, ('tm', 'qband'), split_axis=1, concat_axis=2, ti...  27.1 us
    psum x1, blocking collectives, on_device(): step_size = 1.0 / lax.psum(norm_part, 'qband')  25.1 us
    another operation x2, other arithmetic  24.9 us
  transfers between devices with their start and end apart: 1, of which 1 were waited for; matrix products, arithmetic and copies ran while one was open for 0% of the time, Pallas kernels for 0%

commit v1 on v0

--- a/solution.py
+++ b/solution.py
@@ -76,7 +76,7 @@
     step_size = 1.0 / lax.psum(norm_part, "qband")
 
     def combine_bins(partial_value):
-        return lax.psum(partial_value, "qband")
+        return jnp.sum(lax.all_gather(partial_value, "qband"), axis=0)
 
     def iterate(counter, weights):
         return descend(kernel, target, step_size, weights, combine_bins)

time: 891 us -> 835 us (0.937)
  blocking collectives: 471 us -> 414 us
    psum x64 -> x0, blocking collectives: 381 us -> none  [combine_bins(): return lax.psum(partial_value, 'qband')]
    all_gather x0 -> x64, blocking collectives: none -> 325 us  [combine_bins(): return jnp.sum(lax.all_gather(partial_value, 'qband'), axis=0)]
where the time goes in v1:
time: 835 us; the launch traced here: 833 us
  blocking collectives  414 us (50%)
  other arithmetic  251 us (30%)
  matrix products  51.5 us (6%)
  loops' own time  42.4 us (5%)
  local copies, waits for them, and re-layouts  33.7 us (4%)
  waiting for transfers between devices  27.1 us (3%)
  starting transfers between devices  11.9 us (1%)
    all_gather x64, blocking collectives, combine_bins(): return jnp.sum(lax.all_gather(partial_value, 'qband'), axis=0)  325 us
    sub x16, other arithmetic, one_lag(): shifted.astype(jnp.float32) - spectrum_block.astype(jnp.float32)  142 us
    reduce_sum x16, other arithmetic, one_lag(): summed = jnp.sum(squared * in_range[None, :, None], axis=1)  73.8 us
    psum x1, blocking collectives, on_device(): totals, counts = lax.psum((partial_totals, partial_counts), ('tm', 'qband'))  64.3 us
    another operation x1, loops' own time, structure_block(): return lax.map(one_lag, lag_list)  42.2 us
    all_to_all x1, waiting for transfers between devices, on_device(): lax.all_to_all(spectrum, ('tm', 'qband'), split_axis=1, concat_axis=2, ti...  27.1 us
    psum x1, blocking collectives, on_device(): step_size = 1.0 / lax.psum(norm_part, 'qband')  25.1 us
    another operation x2, other arithmetic  24.9 us
  transfers between devices with their start and end apart: 1, of which 1 were waited for; matrix products, arithmetic and copies ran while one was open for 0% of the time, Pallas kernels for 0%

profile of v1, /device:TPU:1, one launch (start us, length us, event | category | flops | bytes accessed | tf_op | source)
XLA Modules:
  0.0 833.1 jit_solution(6439644070515327992)
XLA Ops:
  0.6 18.3 %multiply_convert_fusion = (bf16[1024,1024]{1,0:T(8,128)(2,1)S(1)}, bf16[1024,1024]{1,0:T(8,128)(2,1)S(1)}) fusion(), kind=kLoop, calls=%fused_computation.49 | loop fusion | flops 26214400 | bytes 4194304 | tf_op jit(solution)/shard_map/convert.3
  23.3 6.4 copy.9
  29.7 22.7 %convolution_bitcast_fusion = f32[2,1024,1,2048]{3,1,0,2:T(8,128)} fusion(bf16[1024,1024]{1,0:T(8,128)(2,1)} %copy-done.3, bf16[1024,1024]{1,0:T(8,128)(2,1)} %copy-done.4, bf16[2,1024,1024]{2,1,0:T(8,128)(2,1)} %bitcast.67, bf16[1,1024,1024]{2,1,0:T(8,128)(2,1)S(1)} %copy-done), kind=kOutput, calls=%fused_computation.32 | convolution fusion | flops 12895387648 | bytes 27262976 | tf_op jit(solution)/shard_map/ckty,yj->cktj/dot_general | solution.py:56
  52.4 6.6 fusion.30
  59.4 6.3 copy.10
  65.7 11.9 %all-to-all-start = ((bf16[2,1024,1,1024]{3,0,2,1:T(2,128)(2,1)}), bf16[2,1024,1,1024]{3,0,2,1:T(2,128)(2,1)}, u32[]{:S(2)}, u32[]{:S(2)}) async-start(bf16[2,1024,1,1024]{3,0,2,1:T(2,128)(2,1)} %copy.10), calls=%async_computation | async-start | bytes 8388608 | tf_op jit(solution)/shard_map/all_to_all | solution.py:61
  77.9 25.1 %psum.21 = f32[2]{0:T(128)S(1)} all-reduce(f32[2]{0:T(128)S(1)} %multiply_reduce_fusion), channel_id=1, replica_groups=mesh['tm'=32,'qband'=4] {'qband'}, use_global_device_ids=true, to_apply=%region_8.9 | all-reduce | flops 2 | bytes 16 | tf_op jit(solution)/shard_map/psum | solution.py:76
  103.1 27.1 %all-to-all-done = bf16[2,1024,1,1024]{3,0,2,1:T(2,128)(2,1)} async-done(((bf16[2,1024,1,1024]{3,0,2,1:T(2,128)(2,1)}), bf16[2,1024,1,1024]{3,0,2,1:T(2,128)(2,1)}, u32[]{:S(2)}, u32[]{:S(2)}) %all-to-all-start) | async-done | bytes 4194336 | tf_op jit(solution)/shard_map/all_to_all | solution.py:61
  139.1 267.7 %while.22 = (s32[]{:T(128)}, f32[16,8,1024]{2,1,0:T(8,128)S(1)}, s32[16]{0:T(128)S(1)}, bf16[2,8,256,1024]{3,2,1,0:T(8,128)(2,1)}, bf16[2,8,128,1024]{3,2,1,0:T(...) while((s32[]{:T(128)}, f32[16,8,1024]{2,1,0:T(8,128)S(1)}, s32[16]{0:T(128)S(1)}, ...), condition=%wide.region_2.3_spmd.clone, body=%wide.region_0.2_spmd.clone.sunk | while | flops 11534599 | bytes 25265328 | solution.py:36
  141.6 8.9 %convert_subtract_fusion.2 = f32[2,8,128,1024]{3,2,1,0:T(8,128)} fusion(bf16[2,8,128,1024]{3,2,1,0:T(8,128)(2,1)} %get-tuple-element.218, bf16[2,8,256,1024]{3,2,1,0:T(8,128)(2,1)} %get-tuple-element.217, s32[]{:T(128)S(6)} %select_n.30), kind=kLoop, calls=%fused_computation.2.clone.1 | loop fusion | flops 6291456 | bytes 16777220 | tf_op jit(solution)/shard_map/while/body/eval_jaxpr/sub | solution.py:30
  158.4 8.9 %convert_subtract_fusion.2 = f32[2,8,128,1024]{3,2,1,0:T(8,128)} fusion(bf16[2,8,128,1024]{3,2,1,0:T(8,128)(2,1)} %get-tuple-element.218, bf16[2,8,256,1024]{3,2,1,0:T(8,128)(2,1)} %get-tuple-element.217, s32[]{:T(128)S(6)} %select_n.30), kind=kLoop, calls=%fused_computation.2.clone.1 | loop fusion | flops 6291456 | bytes 16777220 | tf_op jit(solution)/shard_map/while/body/eval_jaxpr/sub | solution.py:30
  175.1 8.9 %convert_subtract_fusion.2 = f32[2,8,128,1024]{3,2,1,0:T(8,128)} fusion(bf16[2,8,128,1024]{3,2,1,0:T(8,128)(2,1)} %get-tuple-element.218, bf16[2,8,256,1024]{3,2,1,0:T(8,128)(2,1)} %get-tuple-element.217, s32[]{:T(128)S(6)} %select_n.30), kind=kLoop, calls=%fused_computation.2.clone.1 | loop fusion | flops 6291456 | bytes 16777220 | tf_op jit(solution)/shard_map/while/body/eval_jaxpr/sub | solution.py:30
  191.8 8.9 %convert_subtract_fusion.2 = f32[2,8,128,1024]{3,2,1,0:T(8,128)} fusion(bf16[2,8,128,1024]{3,2,1,0:T(8,128)(2,1)} %get-tuple-element.218, bf16[2,8,256,1024]{3,2,1,0:T(8,128)(2,1)} %get-tuple-element.217, s32[]{:T(128)S(6)} %select_n.30), kind=kLoop, calls=%fused_computation.2.clone.1 | loop fusion | flops 6291456 | bytes 16777220 | tf_op jit(solution)/shard_map/while/body/eval_jaxpr/sub | solution.py:30
  208.6 8.9 %convert_subtract_fusion.2 = f32[2,8,128,1024]{3,2,1,0:T(8,128)} fusion(bf16[2,8,128,1024]{3,2,1,0:T(8,128)(2,1)} %get-tuple-element.218, bf16[2,8,256,1024]{3,2,1,0:T(8,128)(2,1)} %get-tuple-element.217, s32[]{:T(128)S(6)} %select_n.30), kind=kLoop, calls=%fused_computation.2.clone.1 | loop fusion | flops 6291456 | bytes 16777220 | tf_op jit(solution)/shard_map/while/body/eval_jaxpr/sub | solution.py:30
  225.3 8.9 %convert_subtract_fusion.2 = f32[2,8,128,1024]{3,2,1,0:T(8,128)} fusion(bf16[2,8,128,1024]{3,2,1,0:T(8,128)(2,1)} %get-tuple-element.218, bf16[2,8,256,1024]{3,2,1,0:T(8,128)(2,1)} %get-tuple-element.217, s32[]{:T(128)S(6)} %select_n.30), kind=kLoop, calls=%fused_computation.2.clone.1 | loop fusion | flops 6291456 | bytes 16777220 | tf_op jit(solution)/shard_map/while/body/eval_jaxpr/sub | solution.py:30
  242.0 8.9 %convert_subtract_fusion.2 = f32[2,8,128,1024]{3,2,1,0:T(8,128)} fusion(bf16[2,8,128,1024]{3,2,1,0:T(8,128)(2,1)} %get-tuple-element.218, bf16[2,8,256,1024]{3,2,1,0:T(8,128)(2,1)} %get-tuple-element.217, s32[]{:T(128)S(6)} %select_n.30), kind=kLoop, calls=%fused_computation.2.clone.1 | loop fusion | flops 6291456 | bytes 16777220 | tf_op jit(solution)/shard_map/while/body/eval_jaxpr/sub | solution.py:30
  258.7 8.9 %convert_subtract_fusion.2 = f32[2,8,128,1024]{3,2,1,0:T(8,128)} fusion(bf16[2,8,128,1024]{3,2,1,0:T(8,128)(2,1)} %get-tuple-element.218, bf16[2,8,256,1024]{3,2,1,0:T(8,128)(2,1)} %get-tuple-element.217, s32[]{:T(128)S(6)} %select_n.30), kind=kLoop, calls=%fused_computation.2.clone.1 | loop fusion | flops 6291456 | bytes 16777220 | tf_op jit(solution)/shard_map/while/body/eval_jaxpr/sub | solution.py:30
  275.5 8.9 %convert_subtract_fusion.2 = f32[2,8,128,1024]{3,2,1,0:T(8,128)} fusion(bf16[2,8,128,1024]{3,2,1,0:T(8,128)(2,1)} %get-tuple-element.218, bf16[2,8,256,1024]{3,2,1,0:T(8,128)(2,1)} %get-tuple-element.217, s32[]{:T(128)S(6)} %select_n.30), kind=kLoop, calls=%fused_computation.2.clone.1 | loop fusion | flops 6291456 | bytes 16777220 | tf_op jit(solution)/shard_map/while/body/eval_jaxpr/sub | solution.py:30
  292.2 8.9 %convert_subtract_fusion.2 = f32[2,8,128,1024]{3,2,1,0:T(8,128)} fusion(bf16[2,8,128,1024]{3,2,1,0:T(8,128)(2,1)} %get-tuple-element.218, bf16[2,8,256,1024]{3,2,1,0:T(8,128)(2,1)} %get-tuple-element.217, s32[]{:T(128)S(6)} %select_n.30), kind=kLoop, calls=%fused_computation.2.clone.1 | loop fusion | flops 6291456 | bytes 16777220 | tf_op jit(solution)/shard_map/while/body/eval_jaxpr/sub | solution.py:30
  308.9 8.9 %convert_subtract_fusion.2 = f32[2,8,128,1024]{3,2,1,0:T(8,128)} fusion(bf16[2,8,128,1024]{3,2,1,0:T(8,128)(2,1)} %get-tuple-element.218, bf16[2,8,256,1024]{3,2,1,0:T(8,128)(2,1)} %get-tuple-element.217, s32[]{:T(128)S(6)} %select_n.30), kind=kLoop, calls=%fused_computation.2.clone.1 | loop fusion | flops 6291456 | bytes 16777220 | tf_op jit(solution)/shard_map/while/body/eval_jaxpr/sub | solution.py:30
  325.7 8.9 %convert_subtract_fusion.2 = f32[2,8,128,1024]{3,2,1,0:T(8,128)} fusion(bf16[2,8,128,1024]{3,2,1,0:T(8,128)(2,1)} %get-tuple-element.218, bf16[2,8,256,1024]{3,2,1,0:T(8,128)(2,1)} %get-tuple-element.217, s32[]{:T(128)S(6)} %select_n.30), kind=kLoop, calls=%fused_computation.2.clone.1 | loop fusion | flops 6291456 | bytes 16777220 | tf_op jit(solution)/shard_map/while/body/eval_jaxpr/sub | solution.py:30
  342.4 8.9 %convert_subtract_fusion.2 = f32[2,8,128,1024]{3,2,1,0:T(8,128)} fusion(bf16[2,8,128,1024]{3,2,1,0:T(8,128)(2,1)} %get-tuple-element.218, bf16[2,8,256,1024]{3,2,1,0:T(8,128)(2,1)} %get-tuple-element.217, s32[]{:T(128)S(6)} %select_n.30), kind=kLoop, calls=%fused_computation.2.clone.1 | loop fusion | flops 6291456 | bytes 16777220 | tf_op jit(solution)/shard_map/while/body/eval_jaxpr/sub | solution.py:30
  359.1 8.9 %convert_subtract_fusion.2 = f32[2,8,128,1024]{3,2,1,0:T(8,128)} fusion(bf16[2,8,128,1024]{3,2,1,0:T(8,128)(2,1)} %get-tuple-element.218, bf16[2,8,256,1024]{3,2,1,0:T(8,128)(2,1)} %get-tuple-element.217, s32[]{:T(128)S(6)} %select_n.30), kind=kLoop, calls=%fused_computation.2.clone.1 | loop fusion | flops 6291456 | bytes 16777220 | tf_op jit(solution)/shard_map/while/body/eval_jaxpr/sub | solution.py:30
  375.9 8.9 %convert_subtract_fusion.2 = f32[2,8,128,1024]{3,2,1,0:T(8,128)} fusion(bf16[2,8,128,1024]{3,2,1,0:T(8,128)(2,1)} %get-tuple-element.218, bf16[2,8,256,1024]{3,2,1,0:T(8,128)(2,1)} %get-tuple-element.217, s32[]{:T(128)S(6)} %select_n.30), kind=kLoop, calls=%fused_computation.2.clone.1 | loop fusion | flops 6291456 | bytes 16777220 | tf_op jit(solution)/shard_map/while/body/eval_jaxpr/sub | solution.py:30
  392.6 8.9 %convert_subtract_fusion.2 = f32[2,8,128,1024]{3,2,1,0:T(8,128)} fusion(bf16[2,8,128,1024]{3,2,1,0:T(8,128)(2,1)} %get-tuple-element.218, bf16[2,8,256,1024]{3,2,1,0:T(8,128)(2,1)} %get-tuple-element.217, s32[]{:T(128)S(6)} %select_n.30), kind=kLoop, calls=%fused_computation.2.clone.1 | loop fusion | flops 6291456 | bytes 16777220 | tf_op jit(solution)/shard_map/while/body/eval_jaxpr/sub | solution.py:30
  407.2 64.3 %all-reduce.1 = (f32[64,16]{1,0:T(8,128)S(1)}, f32[64]{0:T(128)S(1)}) all-reduce(f32[64,16]{1,0:T(8,128)S(1)} %fusion.44, f32[64]{0:T(128)S(1)} %convert_reduce_fusion), channel_id=1, replica_groups=mesh['tm'=32,'qband'=4] {'tm','qband'}, use_global_device_ids=true, to_apply=%region_4.5 | all-reduce | flops 1088 | bytes 8704 | tf_op jit(solution)/shard_map/psum | solution.py:70
  471.6 360.9 %while.23 = (s32[]{:T(128)}, f32[2,256]{1,0:T(2,128)S(1)}, f32[2]{0:T(128)S(1)}, f32[2,16]{1,0:T(2,128)S(1)}, f32[16]{0:T(128)S(1)}, /*index=5*/f32[2,256]{1,0:T(2,128)S(1)}, s32[]{:T(128)}, s32[]{:T(128)}, f32[]{:T(128)}) while((s32[]{:T(128)}, f32[2,256]{1,0:T(2,128)S(1)}, f32[2]{0:T(128)S(1)}, f32[2,16]{1,0:T(2,128)S(1)}, ...), condition=%wide.region_11.12_spmd.clone, body=%wide.region_9.11_spmd.clone.sunk | while | flops 248451 | bytes 20596 | solution.py:84
  471.9 5.5 all-gather.4
  478.0 5.1 all-gather.4
  483.6 5.1 all-gather.4
  489.2 5.1 all-gather.4
  494.9 5.1 all-gather.4
  500.5 5.1 all-gather.4
  506.1 5.1 all-gather.4
  511.8 5.1 all-gather.4
  517.4 5.1 all-gather.4
  523.0 5.1 all-gather.4
  528.7 5.1 all-gather.4
  534.3 5.1 all-gather.4
  539.9 5.1 all-gather.4
  545.5 5.1 all-gather.4
  551.2 5.1 all-gather.4
  556.8 5.1 all-gather.4
  562.4 5.1 all-gather.4
  568.1 5.1 all-gather.4
  573.7 5.1 all-gather.4
  579.3 5.1 all-gather.4
  585.0 5.1 all-gather.4
  590.6 5.1 all-gather.4
  596.2 5.1 all-gather.4
  601.9 5.1 all-gather.4
  607.5 5.1 all-gather.4
  613.1 5.1 all-gather.4
  618.8 5.1 all-gather.4
  624.4 5.1 all-gather.4
  630.0 5.1 all-gather.4
  635.6 5.1 all-gather.4
  641.3 5.1 all-gather.4
  646.9 5.1 all-gather.4
  652.5 5.1 all-gather.4
  658.2 5.1 all-gather.4
  663.8 5.1 all-gather.4
  669.4 5.1 all-gather.4
  675.1 5.1 all-gather.4
  (511 shorter events, 271.1 us)
Async XLA Ops:
  0.6 29.1 %copy-start = (bf16[1,1024,1024]{2,1,0:T(8,128)(2,1)S(1)}, bf16[1,1024,1024]{2,1,0:T(8,128)(2,1)}, u32[]{:S(2)}) copy-start(bf16[1,1024,1024]{2,1,0:T(8,128)(2,1)} %param.8) | copy-start | bytes 6291460
  19.0 1.3 copy-start.3
  19.0 2.0 copy-start.4
  65.7 12.0 %copy-start.7 = (f32[2,256]{1,0:T(2,128)S(1)}, f32[2,256]{1,0:T(2,128)}, u32[]{:S(2)}) copy-start(f32[2,256]{1,0:T(2,128)} %param.11) | copy-start | bytes 6148
  65.7 12.0 %copy-start.8 = (s32[16]{0:T(128)S(1)}, s32[16]{0:T(128)}, u32[]{:S(2)}) copy-start(s32[16]{0:T(128)} %param.9) | copy-start | bytes 196
  65.7 37.3 %copy-start.9 = (s32[8,1]{0,1:T(1,128)S(1)}, s32[8,1]{0,1:T(1,128)}, u32[]{:S(2)}) copy-start(s32[8,1]{0,1:T(1,128)} %param.10) | copy-start | bytes 100
  65.7 64.4 %all-to-all-start = ((bf16[2,1024,1,1024]{3,0,2,1:T(2,128)(2,1)}), bf16[2,1024,1,1024]{3,0,2,1:T(2,128)(2,1)}, u32[]{:S(2)}, u32[]{:S(2)}) async-start(bf16[2,1024,1,1024]{3,0,2,1:T(2,128)(2,1)} %copy.10), calls=%async_computation | async-start | bytes 8388608 | tf_op jit(solution)/shard_map/all_to_all | solution.py:61
  134.6 4.5 copy-start.2
  406.8 425.7 %copy-start.5 = (f32[16,8,1024]{2,1,0:T(8,128)}, f32[16,8,1024]{2,1,0:T(8,128)S(1)}, u32[]{:S(2)}) copy-start(f32[16,8,1024]{2,1,0:T(8,128)S(1)} %get-tuple-element.59) | copy-start | bytes 1572868
  406.8 426.3 %copy-start.1 = (bf16[1,1024,1024]{2,1,0:T(8,128)(2,1)S(1)}, bf16[1,1024,1024]{2,1,0:T(8,128)(2,1)}, u32[]{:S(2)}) copy-start(bf16[1,1024,1024]{2,1,0:T(8,128)(2,1)} %param.8) | copy-start | bytes 6291460
  832.5 0.6 copy-start.6
